TPU v7x, 32 devices: a whole 2x2x4 slice. The times are simulated.
32 devices in a mesh: tm: 2 (over x), prow: 4 (over z), pcol: 4 (over y, core).
Axes of the slice: x: 2, y: 2, z: 4, core: 2. Of those that a mesh axis runs over, the one named last changes fastest.
Arguments:
- signal: bfloat16 [2048, 15360], P(('prow', 'pcol'), 'tm'), may hold values from -8 to 8
- offsets: int32 [4], replicated, may hold values from 0 to 511, as said below
- pair_list: int32 [4, 4, 4, 2], P('prow', 'pcol'), may hold values from 0 to 3, as said below
Outputs:
- correlations: bfloat16 [4, 4, 4, 128, 128, 256], P('prow', 'pcol', None, 'tm')
Inputs may be any that keep to these rules, and one draw needn't show every extreme that they name: `offsets`: some window has the largest offset. `pair_list`: entry (a, b) of cell (r, c) pairs row block r n + a with column block b n + c, n the number of devices of pcol, and the row block's number is never above the column block's; pairs may repeat.
All inputs are finite; a program needn't handle non-finite values.
Results may differ from a plain program's by a relative error of at most 0.0058.
Values may be sent and summed in bfloat16 or wider, within the bound.
No kernel may reach another device: no remote copies, remote signals or barrier semaphores. Data moves between devices by JAX's collectives and lax.ppermute only.
A program may use at most 128 MiB of HBM per device.

v0:
```python
import math
import jax
import jax.numpy as jnp
from jax import lax
from jax.sharding import PartitionSpec as P

WIN = 7680
NF = 384
K0 = 32
LAGS = 256
SPAN = 4
NP = 4
STEP = 3840
HALO = 4352
two_pi = 2.0 * math.pi


def from_behind(value, axis, steps):
    count = lax.axis_size(axis)
    initial, last = (max(0, -steps), min(count, count - steps))
    return lax.ppermute(value, axis, [(source, source + steps) for source in range(initial, last)])


def forward_table():
    sample_idx = jnp.arange(WIN, dtype=jnp.int32)
    freq_bins = K0 + jnp.arange(NF, dtype=jnp.int32)
    wrapped = sample_idx[:, None] * freq_bins[None, :] % WIN
    phase_angle = wrapped.astype(jnp.float32) * (two_pi / WIN)
    taper_curve = 0.5 - 0.5 * jnp.cos(sample_idx.astype(jnp.float32) * (two_pi / WIN))
    cosine = taper_curve[:, None] * jnp.cos(phase_angle)
    sine = -taper_curve[:, None] * jnp.sin(phase_angle)
    return jnp.concatenate([cosine, sine], axis=1).astype(jnp.bfloat16)


def lag_table(count):
    freq_bins = K0 + jnp.arange(NF, dtype=jnp.int32)
    shifted = (jnp.arange(LAGS, dtype=jnp.int32) - LAGS // 2) % WIN
    wrapped = freq_bins[:, None] * shifted[None, :] % WIN
    phase_angle = wrapped.astype(jnp.float32) * (two_pi / WIN)
    factor = 1.0 / math.sqrt(NF * count)
    return jnp.concatenate(
        [jnp.cos(phase_angle) * factor, -jnp.sin(phase_angle) * factor], axis=0
    ).astype(jnp.bfloat16)


def whiten(spectra):
    real_part = spectra[..., :NF]
    imag_part = spectra[..., NF:]
    power_sum = real_part * real_part + imag_part * imag_part
    freq_bins = jnp.arange(NF, dtype=jnp.int32)
    band_matrix = (jnp.abs(freq_bins[:, None] - freq_bins[None, :]) <= SPAN).astype(jnp.float32)
    smooth = jnp.einsum(
        "...f,fg->...g", power_sum, band_matrix, precision=lax.Precision.HIGHEST
    ) / (2 * SPAN + 1)
    water_level = jnp.mean(power_sum, axis=-1, keepdims=True)
    weight = lax.rsqrt(smooth + 0.5 * water_level + 1e-06)
    return (spectra * jnp.concatenate([weight, weight], axis=-1)).astype(jnp.bfloat16)


def cross_pair(row_block, col_block, lags):
    row_real = row_block[..., :NF]
    row_imag = row_block[..., NF:]
    col_both = jnp.concatenate([col_block[..., :NF], col_block[..., NF:]], axis=0)
    row_first = jnp.concatenate([row_real, row_imag], axis=0)
    row_second = jnp.concatenate([row_imag, -row_real], axis=0)
    real_sum = jnp.einsum("wif,wjf->ijf", row_first, col_both, preferred_element_type=jnp.float32)
    imag_sum = jnp.einsum("wif,wjf->ijf", row_second, col_both, preferred_element_type=jnp.float32)
    cross = jnp.concatenate([real_sum, imag_sum], axis=-1).astype(jnp.bfloat16)
    flat = cross.reshape(-1, 2 * NF)
    result = jnp.dot(flat, lags, preferred_element_type=jnp.float32).astype(jnp.bfloat16)
    return result.reshape(row_block.shape[1], col_block.shape[1], LAGS)


def on_device(signal, offsets, pair_list):
    channels_here = signal.shape[0]
    samples_here = signal.shape[1]
    w_dev = samples_here // STEP
    n_tm = lax.axis_size("tm")
    tm_index = lax.axis_index("tm")
    dft_table = forward_table()
    head_samples = signal[:, :HALO]
    next_head = from_behind(head_samples, "tm", -1)
    extended = jnp.concatenate([signal, next_head], axis=1)

    def one_window(window):
        first_sample = window * STEP + offsets[tm_index * w_dev + window]
        segment = lax.dynamic_slice_in_dim(extended, first_sample, WIN, 1)
        return jnp.dot(segment, dft_table, preferred_element_type=jnp.float32)

    spectra = lax.map(one_window, jnp.arange(w_dev, dtype=jnp.int32))
    whitened = whiten(spectra)
    own_piece = whitened[None]
    row_gathered = lax.all_gather(own_piece, ("tm", "pcol"), axis=0, tiled=True)
    col_gathered = lax.all_gather(own_piece, ("tm", "prow"), axis=0, tiled=True)
    row_gathered = row_gathered.reshape(n_tm, -1, w_dev, channels_here, 2 * NF)
    col_gathered = col_gathered.reshape(n_tm, -1, w_dev, channels_here, 2 * NF)
    pick_dim = 1
    lags = lag_table(n_tm * w_dev)
    local_pairs = pair_list[0, 0]
    half_rows = channels_here // n_tm
    first_row = tm_index * half_rows

    def one_pair(pair_index):
        row_pick = local_pairs[pair_index, 0]
        col_pick = local_pairs[pair_index, 1]
        row_whole = lax.dynamic_index_in_dim(row_gathered, row_pick, pick_dim, keepdims=False)
        col_whole = lax.dynamic_index_in_dim(col_gathered, col_pick, pick_dim, keepdims=False)
        row_whole = row_whole.reshape(n_tm * w_dev, channels_here, 2 * NF)
        col_whole = col_whole.reshape(n_tm * w_dev, channels_here, 2 * NF)
        row_block = lax.dynamic_slice_in_dim(row_whole, first_row, half_rows, 1)
        return cross_pair(row_block, col_whole, lags)

    result = lax.map(one_pair, jnp.arange(NP, dtype=jnp.int32))
    return result.reshape(1, 1, NP, half_rows, channels_here, LAGS)


def solution(mesh):
    placed = (P(("prow", "pcol"), "tm"), P(), P("prow", "pcol", None, None))
    return jax.shard_map(
        on_device,
        mesh=mesh,
        in_specs=placed,
        out_specs=P("prow", "pcol", None, "tm", None, None),
        check_vma=False,
    )
```

profile of v0, /device:TPU:0, one launch (start us, length us, event | category | flops | bytes accessed | tf_op | source)
XLA Modules:
  0.0 409.1 jit_solution(12209533261240623052)
XLA Ops:
  9.3 52.4 %multiply_convert_fusion.1 = (bf16[7680,384]{1,0:T(8,128)(2,1)S(1)}, bf16[7680,384]{1,0:T(8,128)(2,1)S(1)}) fusion(s32[384]{0:T(512)S(1)} %iota_add_fusion, f32[7680]{0:T(1024)S(1)} %get-tuple-element.245, f32[7680]{0:T(1024)S(1)} %get-tuple-element.246), kind=kLoop, calls=%fused_computation.36 | loop fusion | flops 38338560 | bytes 11859456 | tf_op jit(solution)/shard_map/convert.8
  61.8 5.0 %pad_maximum_fusion.3 = bf16[7680,768]{1,0:T(8,128)(2,1)} fusion(bf16[7680,384]{1,0:T(8,128)(2,1)S(1)} %get-tuple-element.244, bf16[7680,384]{1,0:T(8,128)(2,1)S(1)} %get-tuple-element.243), kind=kLoop, calls=%fused_computation.34 | loop fusion | flops 23592960 | bytes 23592960 | tf_op jit(solution)/shard_map/concatenate | solution.py:32
  68.2 19.9 %while.24 = (s32[]{:T(128)}, f32[2,128,768]{2,1,0:T(8,128)}, s32[2]{0:T(128)S(1)}, s32[]{:T(128)}, s32[4]{0:T(128)S(1)}, /*index=5*/bf16[128,12032]{1,0:T(8,128)...) while((s32[]{:T(128)}, f32[2,128,768]{2,1,0:T(8,128)}, ...), condition=%wide.region_1.2_spmd, body=%wide.region_0.1_spmd.sunk | while | flops 1509949440 | bytes 14156537 | solution.py:90
  71.2 7.0 %fusion.61 = f32[2,128,768]{2,1,0:T(8,128)} fusion(f32[2,128,768]{2,1,0:T(8,128)} %get-tuple-element.370, s32[]{:T(128)} %get-tuple-element.369, bf16[7680,768]{1,0:T(8,128)(2,1)} %get-tuple-element.387, bf16[128,12032]{1,0:T(8,128)(2,1)S(1)} %get-tuple-element.386, s32[]{:T(128)S(6)} %select_n.90), kind=kOutput, calls=%fused_computation.3.clone.1 | convolution fusion | flops 1509949440 | bytes 14156292 | tf_op jit(solution)/shard_map/while/body/eval_jaxpr/dot_general | solution.py:88
  81.2 6.9 %fusion.61 = f32[2,128,768]{2,1,0:T(8,128)} fusion(f32[2,128,768]{2,1,0:T(8,128)} %get-tuple-element.370, s32[]{:T(128)} %get-tuple-element.369, bf16[7680,768]{1,0:T(8,128)(2,1)} %get-tuple-element.387, bf16[128,12032]{1,0:T(8,128)(2,1)S(1)} %get-tuple-element.386, s32[]{:T(128)S(6)} %select_n.90), kind=kOutput, calls=%fused_computation.3.clone.1 | convolution fusion | flops 1509949440 | bytes 14156292 | tf_op jit(solution)/shard_map/while/body/eval_jaxpr/dot_general | solution.py:88
  95.9 62.2 %all-gather.5.cloned.1.call-done = bf16[16,128,768]{2,1,0:T(8,128)(2,1)} async-done(((bf16[2,128,768]{2,1,0:T(8,128)(2,1)}), bf16[16,128,768]{2,1,0:T(8,128)(2,1)}) %all-gather.5.cloned.1.call-update) | async-done | bytes 3145744 | tf_op jit(solution)/shard_map/all_gather | solution.py:94
  158.1 32.8 %all-gather.7.cloned.1.call-done = bf16[16,128,768]{2,1,0:T(8,128)(2,1)} async-done(((bf16[2,128,768]{2,1,0:T(8,128)(2,1)}), bf16[16,128,768]{2,1,0:T(8,128)(2,1)}) %all-gather.7.cloned.1.call-update) | async-done | bytes 3145744 | tf_op jit(solution)/shard_map/all_gather | solution.py:93
  190.9 211.1 %while.25 = (s32[]{:T(128)}, bf16[4,64,128,256]{3,2,1,0:T(8,128)(2,1)}, s32[4]{0:T(128)S(1)}, s32[4,2]{0,1:T(2,128)S(1)}, bf16[2,4,2,128,768]{4,3,2,1,0:T(8,128)...) while((s32[]{:T(128)}, ...), condition=%wide.region_4.5_spmd, body=%wide.region_3.4_spmd.sunk | while | flops 3360456704 | bytes 74515224 | solution.py:113
  224.5 12.5 %copy.23 = bf16[48,8,64,128]{3,1,2,0:T(8,128)(2,1)S(1)} copy(bf16[48,8,64,128]{3,2,1,0:T(8,128)(2,1)S(1)} %bitcast.66) | data formatting | bytes 12582912 | tf_op jit(solution)/shard_map/while
  239.1 12.5 %copy.22 = bf16[48,8,64,128]{3,1,2,0:T(8,128)(2,1)S(1)} copy(bf16[48,8,64,128]{3,2,1,0:T(8,128)(2,1)S(1)} %bitcast.65) | data formatting | bytes 12582912 | tf_op jit(solution)/shard_map/while
  251.6 5.6 %fusion.68 = bf16[8192,256]{1,0:T(8,128)(2,1)S(1)} fusion(bf16[768,256]{1,0:T(8,128)(2,1)S(1)} %get-tuple-element.424, bf16[8192,384]{0,1:T(8,128)(2,1)S(1)} %bitcast.68, bf16[8192,384]{0,1:T(8,128)(2,1)S(1)} %bitcast.67), kind=kOutput, calls=%fused_computation.9.clone.1 | convolution fusion | flops 3248488448 | bytes 17170432 | tf_op jit(solution)/shard_map/while/body/eval_jaxpr/dot_general | solution.py:70
  257.2 2.3 constant_dynamic-update-slice_fusion.2
  272.0 12.5 %copy.23 = bf16[48,8,64,128]{3,1,2,0:T(8,128)(2,1)S(1)} copy(bf16[48,8,64,128]{3,2,1,0:T(8,128)(2,1)S(1)} %bitcast.66) | data formatting | bytes 12582912 | tf_op jit(solution)/shard_map/while
  286.6 12.5 %copy.22 = bf16[48,8,64,128]{3,1,2,0:T(8,128)(2,1)S(1)} copy(bf16[48,8,64,128]{3,2,1,0:T(8,128)(2,1)S(1)} %bitcast.65) | data formatting | bytes 12582912 | tf_op jit(solution)/shard_map/while
  299.1 5.6 %fusion.68 = bf16[8192,256]{1,0:T(8,128)(2,1)S(1)} fusion(bf16[768,256]{1,0:T(8,128)(2,1)S(1)} %get-tuple-element.424, bf16[8192,384]{0,1:T(8,128)(2,1)S(1)} %bitcast.68, bf16[8192,384]{0,1:T(8,128)(2,1)S(1)} %bitcast.67), kind=kOutput, calls=%fused_computation.9.clone.1 | convolution fusion | flops 3248488448 | bytes 17170432 | tf_op jit(solution)/shard_map/while/body/eval_jaxpr/dot_general | solution.py:70
  304.7 2.3 constant_dynamic-update-slice_fusion.2
  319.5 12.5 %copy.23 = bf16[48,8,64,128]{3,1,2,0:T(8,128)(2,1)S(1)} copy(bf16[48,8,64,128]{3,2,1,0:T(8,128)(2,1)S(1)} %bitcast.66) | data formatting | bytes 12582912 | tf_op jit(solution)/shard_map/while
  334.1 12.5 %copy.22 = bf16[48,8,64,128]{3,1,2,0:T(8,128)(2,1)S(1)} copy(bf16[48,8,64,128]{3,2,1,0:T(8,128)(2,1)S(1)} %bitcast.65) | data formatting | bytes 12582912 | tf_op jit(solution)/shard_map/while
  346.6 5.6 %fusion.68 = bf16[8192,256]{1,0:T(8,128)(2,1)S(1)} fusion(bf16[768,256]{1,0:T(8,128)(2,1)S(1)} %get-tuple-element.424, bf16[8192,384]{0,1:T(8,128)(2,1)S(1)} %bitcast.68, bf16[8192,384]{0,1:T(8,128)(2,1)S(1)} %bitcast.67), kind=kOutput, calls=%fused_computation.9.clone.1 | convolution fusion | flops 3248488448 | bytes 17170432 | tf_op jit(solution)/shard_map/while/body/eval_jaxpr/dot_general | solution.py:70
  352.2 2.3 constant_dynamic-update-slice_fusion.2
  366.9 12.5 %copy.23 = bf16[48,8,64,128]{3,1,2,0:T(8,128)(2,1)S(1)} copy(bf16[48,8,64,128]{3,2,1,0:T(8,128)(2,1)S(1)} %bitcast.66) | data formatting | bytes 12582912 | tf_op jit(solution)/shard_map/while
  381.6 12.5 %copy.22 = bf16[48,8,64,128]{3,1,2,0:T(8,128)(2,1)S(1)} copy(bf16[48,8,64,128]{3,2,1,0:T(8,128)(2,1)S(1)} %bitcast.65) | data formatting | bytes 12582912 | tf_op jit(solution)/shard_map/while
  394.1 5.6 %fusion.68 = bf16[8192,256]{1,0:T(8,128)(2,1)S(1)} fusion(bf16[768,256]{1,0:T(8,128)(2,1)S(1)} %get-tuple-element.424, bf16[8192,384]{0,1:T(8,128)(2,1)S(1)} %bitcast.68, bf16[8192,384]{0,1:T(8,128)(2,1)S(1)} %bitcast.67), kind=kOutput, calls=%fused_computation.9.clone.1 | convolution fusion | flops 3248488448 | bytes 17170432 | tf_op jit(solution)/shard_map/while/body/eval_jaxpr/dot_general | solution.py:70
  399.6 2.3 constant_dynamic-update-slice_fusion.2
  (67 shorter events, 50.9 us)
Async XLA Ops:
  6.5 151.5 %all-gather.5.cloned.1.call-start = ((), (), s32[]{:S(2)}) async-start(), calls=%async_computation | async-start | bytes 3538944 | tf_op jit(solution)/shard_map/all_gather | solution.py:94
  7.9 58.9 %collective-permute-start = (bf16[128,4352]{1,0:T(8,128)(2,1)S(1)}, bf16[128,4352]{1,0:T(8,128)(2,1)}, u32[]{:S(2)}, u32[]{:S(2)}) collective-permute-start(bf16[128,4352]{1,0:T(8,128)(2,1)S(1)} %slice.29), channel_id=1, source_target_pairs={{16,0},{17,1},{18,2},{19,3},{20,4},{21,5},{22,6},{23,7},{24,8},{25... | collective-permute-start | bytes 3342344 | tf_op jit(solution)/shard_map/ppermute | solution.py:21
  61.8 5.0 %copy-start = (bf16[128,7680]{1,0:T(8,128)(2,1)S(1)}, bf16[128,7680]{1,0:T(8,128)(2,1)}, u32[]{:S(2)}) copy-start(bf16[128,7680]{1,0:T(8,128)(2,1)} %param.7) | copy-start | bytes 5898244
  61.8 6.4 %copy-start.2 = (s32[4]{0:T(128)S(1)}, s32[4]{0:T(128)}, u32[]{:S(2)}) copy-start(s32[4]{0:T(128)} %param.8) | copy-start | bytes 52
  68.2 122.6 %copy-start.1 = (s32[1,1,4,2]{2,3,1,0:T(2,128)S(1)}, s32[1,1,4,2]{2,3,1,0:T(2,128)}, u32[]{:S(2)}) copy-start(s32[1,1,4,2]{2,3,1,0:T(2,128)} %param.9) | copy-start | bytes 100
  93.1 97.7 %all-gather.7.cloned.1.call-start = ((), (), s32[]{:S(2)}) async-start(), calls=%async_computation.1 | async-start | bytes 3538944 | tf_op jit(solution)/shard_map/all_gather | solution.py:93
Sparse Core Ops, SparseCore 0:
  93.2 64.8 all-gather.4
  160.0 30.8 all-gather.6
where the time goes:
time: 415 us; the launch traced here: 409 us
  local copies, waits for them, and re-layouts  130 us (31%)
  waiting for transfers between devices  95.7 us (23%)
  other arithmetic  66.6 us (16%)
  matrix products  55.2 us (13%)
  loops' own time  46.9 us (11%)
  between operations  13.9 us (3%)
    while x8, local copies, waits for them, and re-layouts  99.7 us
    all_gather x1, waiting for transfers between devices, on_device(): col_gathered = lax.all_gather(own_piece, ('tm', 'prow'), axis=0, tiled=True)  62.2 us
    another operation x2, other arithmetic  54.4 us
    another operation x1, loops' own time, on_device(): result = lax.map(one_pair, jnp.arange(NP, dtype=jnp.int32))  43.2 us
    all_gather x1, waiting for transfers between devices, on_device(): row_gathered = lax.all_gather(own_piece, ('tm', 'pcol'), axis=0, tiled=True)  32.8 us
    dot_general x4, matrix products, cross_pair(): jnp.dot(flat, lags, preferred_element_type=jnp.float32).astype(jnp.bfloat16)  22.3 us
    dot_general x2, matrix products, one_window(): return jnp.dot(segment, dft_table, preferred_element_type=jnp.float32)  13.9 us
    dynamic_update_slice x4, local copies, waits for them, and re-layouts, on_device(): result = lax.map(one_pair, jnp.arange(NP, dtype=jnp.int32))  9.16 us
  transfers between devices with their start and end apart: 3, of which 2 were waited for; matrix products, arithmetic and copies ran while one was open for 15% of the time, Pallas kernels for 0%

commit v1 on v0

--- a/solution.py
+++ b/solution.py
@@ -3,6 +3,7 @@
 import jax.numpy as jnp
 from jax import lax
 from jax.sharding import PartitionSpec as P
+from jax.lax import axis_index, axis_size, ppermute
 
 WIN = 7680
 NF = 384
@@ -13,6 +14,22 @@
 STEP = 3840
 HALO = 4352
 two_pi = 2.0 * math.pi
+
+
+def track_surface(slab_in):
+    main = axis_size(("tm", "pcol"))
+    x_next = axis_index(("tm", "pcol"))
+    parts_out, opened = (main, x_next)
+    long_array, local_next = (slab_in, 1)
+    while local_next < parts_out:
+        upper = ppermute(
+            long_array, ("tm", "pcol"), [(num, num ^ local_next) for num in range(parts_out)]
+        )
+        field_out = jnp.concatenate([long_array, upper], axis=0)
+        y_new = jnp.concatenate([upper, long_array], axis=0)
+        long_array = jnp.where(opened & local_next == 0, field_out, y_new)
+        local_next = 2 * local_next
+    return long_array
 
 
 def from_behind(value, axis, steps):
@@ -90,7 +107,7 @@
     spectra = lax.map(one_window, jnp.arange(w_dev, dtype=jnp.int32))
     whitened = whiten(spectra)
     own_piece = whitened[None]
-    row_gathered = lax.all_gather(own_piece, ("tm", "pcol"), axis=0, tiled=True)
+    row_gathered = track_surface(own_piece)
     col_gathered = lax.all_gather(own_piece, ("tm", "prow"), axis=0, tiled=True)
     row_gathered = row_gathered.reshape(n_tm, -1, w_dev, channels_here, 2 * NF)
     col_gathered = col_gathered.reshape(n_tm, -1, w_dev, channels_here, 2 * NF)

time: 415 us -> 400 us (0.964)
  waiting for transfers between devices: 95.7 us -> 69.6 us
  starting transfers between devices: 1.34 us -> 8.45 us
    ppermute x0 -> x3, waiting for transfers between devices: none -> 68.5 us  [track_surface(): ppermute(long_array, ('tm', 'pcol'), [(num, num ^ local_next) for num in...]
    all_gather x1, waiting for transfers between devices: 62.2 us -> 1.07 us  [on_device(): col_gathered = lax.all_gather(own_piece, ('tm', 'prow'), axis=0, tiled=True)]
    all_gather x1 -> x0, waiting for transfers between devices: 32.8 us -> none  [on_device(): row_gathered = lax.all_gather(own_piece, ('tm', 'pcol'), axis=0, tiled=True)]
    ppermute x0 -> x3, starting transfers between devices: none -> 7.16 us  [track_surface(): ppermute(long_array, ('tm', 'pcol'), [(num, num ^ local_next) for num in...]
  transfers between devices with their start and end apart: 3 -> 5, of which waited for: 2 -> 4; matrix products, arithmetic and copies ran while one was open for 15% -> 16% of each run, Pallas kernels for 0% -> 0%
where the time goes in v1:
time: 400 us; the launch traced here: 393 us
  local copies, waits for them, and re-layouts  130 us (32%)
  other arithmetic  70 us (18%)
  waiting for transfers between devices  69.6 us (17%)
  matrix products  55.1 us (14%)
  loops' own time  46.9 us (12%)
  between operations  13.9 us (3%)
  starting transfers between devices  8.45 us (2%)
    while x8, local copies, waits for them, and re-layouts  99.7 us
    ppermute x3, waiting for transfers between devices, track_surface(): ppermute(long_array, ('tm', 'pcol'), [(num, num ^ local_next) for num in...  68.5 us
    another operation x2, other arithmetic  54.4 us
    another operation x1, loops' own time, on_device(): result = lax.map(one_pair, jnp.arange(NP, dtype=jnp.int32))  43.2 us
    dot_general x4, matrix products, cross_pair(): jnp.dot(flat, lags, preferred_element_type=jnp.float32).astype(jnp.bfloat16)  22.2 us
    dot_general x2, matrix products, one_window(): return jnp.dot(segment, dft_table, preferred_element_type=jnp.float32)  13.9 us
    dynamic_update_slice x4, local copies, waits for them, and re-layouts, on_device(): result = lax.map(one_pair, jnp.arange(NP, dtype=jnp.int32))  9.16 us
    dot_general x4, matrix products, cross_pair(): jnp.einsum('wif,wjf->ijf', row_second, col_both, preferred_element_type=j...  8.64 us
  transfers between devices with their start and end apart: 5, of which 4 were waited for; matrix products, arithmetic and copies ran while one was open for 16% of the time, Pallas kernels for 0%

profile of v1, /device:TPU:0, one launch (start us, length us, event | category | flops | bytes accessed | tf_op | source)
XLA Modules:
  0.0 393.5 jit_solution(9847121963589465245)
XLA Ops:
  9.3 52.4 %multiply_convert_fusion.1 = (bf16[7680,384]{1,0:T(8,128)(2,1)S(1)}, bf16[7680,384]{1,0:T(8,128)(2,1)S(1)}) fusion(s32[384]{0:T(512)S(1)} %iota_add_fusion, f32[7680]{0:T(1024)S(1)} %get-tuple-element.245, f32[7680]{0:T(1024)S(1)} %get-tuple-element.246), kind=kLoop, calls=%fused_computation.36 | loop fusion | flops 38338560 | bytes 11859456 | tf_op jit(solution)/shard_map/convert.8
  61.8 5.0 %pad_maximum_fusion.3 = bf16[7680,768]{1,0:T(8,128)(2,1)} fusion(bf16[7680,384]{1,0:T(8,128)(2,1)S(1)} %get-tuple-element.244, bf16[7680,384]{1,0:T(8,128)(2,1)S(1)} %get-tuple-element.243), kind=kLoop, calls=%fused_computation.34 | loop fusion | flops 23592960 | bytes 23592960 | tf_op jit(solution)/shard_map/concatenate | solution.py:49
  68.2 19.9 %while.24 = (s32[]{:T(128)}, f32[2,128,768]{2,1,0:T(8,128)}, s32[2]{0:T(128)S(1)}, s32[]{:T(128)}, s32[4]{0:T(128)S(1)}, /*index=5*/bf16[128,12032]{1,0:T(8,128)...) while((s32[]{:T(128)}, f32[2,128,768]{2,1,0:T(8,128)}, ...), condition=%wide.region_1.2_spmd, body=%wide.region_0.1_spmd.sunk | while | flops 1509949440 | bytes 14156537 | solution.py:107
  71.2 7.0 %fusion.61 = f32[2,128,768]{2,1,0:T(8,128)} fusion(f32[2,128,768]{2,1,0:T(8,128)} %get-tuple-element.370, s32[]{:T(128)} %get-tuple-element.369, bf16[7680,768]{1,0:T(8,128)(2,1)} %get-tuple-element.387, bf16[128,12032]{1,0:T(8,128)(2,1)S(1)} %get-tuple-element.386, s32[]{:T(128)S(6)} %select_n.131), kind=kOutput, calls=%fused_computation.3.clone.1 | convolution fusion | flops 1509949440 | bytes 14156292 | tf_op jit(solution)/shard_map/while/body/eval_jaxpr/dot_general | solution.py:105
  81.2 6.9 %fusion.61 = f32[2,128,768]{2,1,0:T(8,128)} fusion(f32[2,128,768]{2,1,0:T(8,128)} %get-tuple-element.370, s32[]{:T(128)} %get-tuple-element.369, bf16[7680,768]{1,0:T(8,128)(2,1)} %get-tuple-element.387, bf16[128,12032]{1,0:T(8,128)(2,1)S(1)} %get-tuple-element.386, s32[]{:T(128)S(6)} %select_n.131), kind=kOutput, calls=%fused_computation.3.clone.1 | convolution fusion | flops 1509949440 | bytes 14156292 | tf_op jit(solution)/shard_map/while/body/eval_jaxpr/dot_general | solution.py:105
  96.4 3.0 collective-permute-start.2
  99.4 17.8 %collective-permute-done.2 = bf16[2,2,128,768]{3,2,1,0:T(8,128)(2,1)S(1)} collective-permute-done((bf16[2,2,128,768]{3,2,1,0:T(8,128)(2,1)S(1)}, bf16[2,2,128,768]{3,2,1,0:T(8,128)(2,1)S(1)}, u32[]{:S(2)}, u32[]{:S(2)}) %collective-permute-start.2) | collective-permute-done | bytes 786464 | tf_op jit(solution)/shard_map/ppermute | solution.py:25
  117.5 3.6 collective-permute-start.3
  123.1 49.1 %collective-permute-done.3 = bf16[4,2,128,768]{3,2,1,0:T(8,128)(2,1)S(1)} collective-permute-done((bf16[4,2,128,768]{3,2,1,0:T(8,128)(2,1)S(1)}, bf16[4,2,128,768]{3,2,1,0:T(8,128)(2,1)S(1)}, u32[]{:S(2)}, u32[]{:S(2)}) %collective-permute-start.3) | collective-permute-done | bytes 1572896 | tf_op jit(solution)/shard_map/ppermute | solution.py:25
  175.2 211.0 %while.25 = (s32[]{:T(128)}, bf16[4,64,128,256]{3,2,1,0:T(8,128)(2,1)}, s32[4]{0:T(128)S(1)}, s32[4,2]{0,1:T(2,128)S(1)}, bf16[2,4,2,128,768]{4,3,2,1,0:T(8,128)...) while((s32[]{:T(128)}, ...), condition=%wide.region_4.5_spmd, body=%wide.region_3.4_spmd.sunk | while | flops 3360456704 | bytes 74515224 | solution.py:130
  208.8 12.5 %copy.23 = bf16[48,8,64,128]{3,1,2,0:T(8,128)(2,1)S(1)} copy(bf16[48,8,64,128]{3,2,1,0:T(8,128)(2,1)S(1)} %bitcast.67) | data formatting | bytes 12582912 | tf_op jit(solution)/shard_map/while
  223.5 12.5 %copy.22 = bf16[48,8,64,128]{3,1,2,0:T(8,128)(2,1)S(1)} copy(bf16[48,8,64,128]{3,2,1,0:T(8,128)(2,1)S(1)} %bitcast.66) | data formatting | bytes 12582912 | tf_op jit(solution)/shard_map/while
  236.0 5.6 %fusion.68 = bf16[8192,256]{1,0:T(8,128)(2,1)S(1)} fusion(bf16[768,256]{1,0:T(8,128)(2,1)S(1)} %get-tuple-element.424, bf16[8192,384]{0,1:T(8,128)(2,1)S(1)} %bitcast.69, bf16[8192,384]{0,1:T(8,128)(2,1)S(1)} %bitcast.68), kind=kOutput, calls=%fused_computation.9.clone.1 | convolution fusion | flops 3248488448 | bytes 17170432 | tf_op jit(solution)/shard_map/while/body/eval_jaxpr/dot_general | solution.py:87
  241.5 2.3 constant_dynamic-update-slice_fusion.2
  256.3 12.5 %copy.23 = bf16[48,8,64,128]{3,1,2,0:T(8,128)(2,1)S(1)} copy(bf16[48,8,64,128]{3,2,1,0:T(8,128)(2,1)S(1)} %bitcast.67) | data formatting | bytes 12582912 | tf_op jit(solution)/shard_map/while
  271.0 12.5 %copy.22 = bf16[48,8,64,128]{3,1,2,0:T(8,128)(2,1)S(1)} copy(bf16[48,8,64,128]{3,2,1,0:T(8,128)(2,1)S(1)} %bitcast.66) | data formatting | bytes 12582912 | tf_op jit(solution)/shard_map/while
  283.4 5.6 %fusion.68 = bf16[8192,256]{1,0:T(8,128)(2,1)S(1)} fusion(bf16[768,256]{1,0:T(8,128)(2,1)S(1)} %get-tuple-element.424, bf16[8192,384]{0,1:T(8,128)(2,1)S(1)} %bitcast.69, bf16[8192,384]{0,1:T(8,128)(2,1)S(1)} %bitcast.68), kind=kOutput, calls=%fused_computation.9.clone.1 | convolution fusion | flops 3248488448 | bytes 17170432 | tf_op jit(solution)/shard_map/while/body/eval_jaxpr/dot_general | solution.py:87
  303.8 12.5 %copy.23 = bf16[48,8,64,128]{3,1,2,0:T(8,128)(2,1)S(1)} copy(bf16[48,8,64,128]{3,2,1,0:T(8,128)(2,1)S(1)} %bitcast.67) | data formatting | bytes 12582912 | tf_op jit(solution)/shard_map/while
  318.4 12.5 %copy.22 = bf16[48,8,64,128]{3,1,2,0:T(8,128)(2,1)S(1)} copy(bf16[48,8,64,128]{3,2,1,0:T(8,128)(2,1)S(1)} %bitcast.66) | data formatting | bytes 12582912 | tf_op jit(solution)/shard_map/while
  330.9 5.6 %fusion.68 = bf16[8192,256]{1,0:T(8,128)(2,1)S(1)} fusion(bf16[768,256]{1,0:T(8,128)(2,1)S(1)} %get-tuple-element.424, bf16[8192,384]{0,1:T(8,128)(2,1)S(1)} %bitcast.69, bf16[8192,384]{0,1:T(8,128)(2,1)S(1)} %bitcast.68), kind=kOutput, calls=%fused_computation.9.clone.1 | convolution fusion | flops 3248488448 | bytes 17170432 | tf_op jit(solution)/shard_map/while/body/eval_jaxpr/dot_general | solution.py:87
  336.5 2.3 constant_dynamic-update-slice_fusion.2
  351.3 12.5 %copy.23 = bf16[48,8,64,128]{3,1,2,0:T(8,128)(2,1)S(1)} copy(bf16[48,8,64,128]{3,2,1,0:T(8,128)(2,1)S(1)} %bitcast.67) | data formatting | bytes 12582912 | tf_op jit(solution)/shard_map/while
  365.9 12.5 %copy.22 = bf16[48,8,64,128]{3,1,2,0:T(8,128)(2,1)S(1)} copy(bf16[48,8,64,128]{3,2,1,0:T(8,128)(2,1)S(1)} %bitcast.66) | data formatting | bytes 12582912 | tf_op jit(solution)/shard_map/while
  378.4 5.6 %fusion.68 = bf16[8192,256]{1,0:T(8,128)(2,1)S(1)} fusion(bf16[768,256]{1,0:T(8,128)(2,1)S(1)} %get-tuple-element.424, bf16[8192,384]{0,1:T(8,128)(2,1)S(1)} %bitcast.69, bf16[8192,384]{0,1:T(8,128)(2,1)S(1)} %bitcast.68), kind=kOutput, calls=%fused_computation.9.clone.1 | convolution fusion | flops 3248488448 | bytes 17170432 | tf_op jit(solution)/shard_map/while/body/eval_jaxpr/dot_general | solution.py:87
  (73 shorter events, 61.3 us)
Async XLA Ops:
  6.5 168.7 %all-gather.3.cloned.1.call-start = ((), (), s32[]{:S(2)}) async-start(), calls=%async_computation | async-start | bytes 3538944 | tf_op jit(solution)/shard_map/all_gather | solution.py:111
  7.9 58.9 %collective-permute-start = (bf16[128,4352]{1,0:T(8,128)(2,1)S(1)}, bf16[128,4352]{1,0:T(8,128)(2,1)}, u32[]{:S(2)}, u32[]{:S(2)}) collective-permute-start(bf16[128,4352]{1,0:T(8,128)(2,1)S(1)} %slice.29), channel_id=1, source_target_pairs={{16,0},{17,1},{18,2},{19,3},{20,4},{21,5},{22,6},{23,7},{24,8},{25... | collective-permute-start | bytes 3342344 | tf_op jit(solution)/shard_map/ppermute | solution.py:38
  61.8 5.0 %copy-start = (bf16[128,7680]{1,0:T(8,128)(2,1)S(1)}, bf16[128,7680]{1,0:T(8,128)(2,1)}, u32[]{:S(2)}) copy-start(bf16[128,7680]{1,0:T(8,128)(2,1)} %param.7) | copy-start | bytes 5898244
  66.7 1.5 copy-start.2
  93.1 2.1 collective-permute-start.1
  93.6 81.6 %copy-start.1 = (s32[1,1,4,2]{2,3,1,0:T(2,128)S(1)}, s32[1,1,4,2]{2,3,1,0:T(2,128)}, u32[]{:S(2)}) copy-start(s32[1,1,4,2]{2,3,1,0:T(2,128)} %param.9) | copy-start | bytes 100
  96.4 20.8 %collective-permute-start.2 = (bf16[2,2,128,768]{3,2,1,0:T(8,128)(2,1)S(1)}, bf16[2,2,128,768]{3,2,1,0:T(8,128)(2,1)S(1)}, u32[]{:S(2)}, u32[]{:S(2)}) collective-permute-start(bf16[2,2,128,768]{3,2,1,0:T(8,128)(2,1)S(1)} %maximum_select_fusion.2), channel_id=1, source_target_pairs={{0,2},{1,3},{2,0},{3,1},{16,18},{17,19},{18,16},{19,17},{4,6},{5,7... | collective-permute-start | bytes 2359304 | tf_op jit(solution)/shard_map/ppermute | solution.py:25
  117.5 54.7 %collective-permute-start.3 = (bf16[4,2,128,768]{3,2,1,0:T(8,128)(2,1)S(1)}, bf16[4,2,128,768]{3,2,1,0:T(8,128)(2,1)S(1)}, u32[]{:S(2)}, u32[]{:S(2)}) collective-permute-start(bf16[4,2,128,768]{3,2,1,0:T(8,128)(2,1)S(1)} %maximum_select_fusion.1), channel_id=1, source_target_pairs={{0,16},{1,17},{2,18},{3,19},{16,0},{17,1},{18,2},{19,3},{4,20},{5,... | collective-permute-start | bytes 4718600 | tf_op jit(solution)/shard_map/ppermute | solution.py:25
Sparse Core Ops, SparseCore 0:
  93.2 81.9 all-gather.2
